TPU v7x, 32 devices: a whole 2x2x4 slice. The times are simulated.
32 devices in a mesh: seq: 8 (over z, x), exp: 4 (over y, core).
Axes of the slice: x: 2, y: 2, z: 4, core: 2. Of those that a mesh axis runs over, the one named last changes fastest.
Arguments:
- hidden_in: bfloat16 [2048, 1536], P('seq'), may hold values from -6 to 6
- attn_gain: float32 [1536], replicated, may hold values from 0.1 to 1.9
- q_weight: bfloat16 [1536, 1536], P(None, 'exp'), may hold values from -1.25 to 1.25
- k_weight: bfloat16 [1536, 512], P(None, 'exp'), may hold values from -0.625 to 0.625
- v_weight: bfloat16 [1536, 512], P(None, 'exp'), may hold values from -0.15625 to 0.15625
- o_weight: bfloat16 [1536, 1536], P('exp'), may hold values from -0.15625 to 0.15625
- cache_kv: bfloat16 [4096, 1024], P('seq', 'exp'), may hold values from -216 to 216
- moe_gain: float32 [1536], replicated, may hold values from 0.1 to 1.9
- expert_in: bfloat16 [32, 1536, 1024], P('seq'), may hold values from -0.15625 to 0.15625
- expert_out: bfloat16 [32, 512, 1536], P('seq'), may hold values from -0.25 to 0.25
- routes: int32 [2048, 8], P(('seq', 'exp')), may hold values from 0 to 31, all different within a row; in each aligned block of 64 rows (0 to 63, 64 to 127, ...) at most 32 rows name the same one
- route_prob: float32 [2048, 8], P(('seq', 'exp')), may hold values from 0.05 to 1
- page_slot: int32 [256], replicated, may hold values from 0 to 31, as said below
Outputs:
- hidden_out: bfloat16 [2048, 1536], P(('seq', 'exp'))
- decode_pages: bfloat16 [256, 8, 2, 512], P('seq', 'exp')
Inputs may be any that keep to these rules, and one draw needn't show every extreme that they name: `routes`: in each aligned block of 64 rows (the rows of one device) no expert is named by more than 32 rows; a row names 8 different experts. `page_slot`: for each r, the 32 blocks b with b mod (8) == r have different slots.
All inputs are finite; a program needn't handle non-finite values.
Results may differ from a plain program's by a relative error of at most 0.0074.
Values may be sent and summed in bfloat16 or wider, within the bound.
No kernel may reach another device: no remote copies, remote signals or barrier semaphores. Data moves between devices by JAX's collectives and lax.ppermute only.
A program may use at most 128 MiB of HBM per device.

v0:
```python
import math
import jax
import jax.numpy as jnp
from jax import lax
from jax.sharding import PartitionSpec as P

HEADS = 24
KV_HEADS = 8
HEAD_DIM = 64
EXPERTS = 32
PAGE = 8
norm_epsilon = 1e-06
attention_scale = 0.015625
residual_scale = 0.22
masked_score = -1e30


def rms_norm(values, gain_row):
    widened = values.astype(jnp.float32)
    spread = lax.rsqrt(jnp.mean(widened * widened, axis=-1, keepdims=True) + norm_epsilon)
    return (widened * spread * gain_row).astype(jnp.bfloat16)


def attend_block(carried, query_heads, visible, key_rows, value_rows):
    best_old, total_old, summed_old = carried
    scores = (
        jnp.einsum("tkgd,nkd->kgtn", query_heads, key_rows, preferred_element_type=jnp.float32)
        * attention_scale
    )
    scores = jnp.where(visible, scores, masked_score)
    best_new = jnp.maximum(best_old, jnp.max(scores, axis=-1))
    weights = jnp.where(visible, jnp.exp(scores - best_new[..., None]), 0.0)
    factor = jnp.exp(best_old - best_new)
    total_new = total_old * factor + jnp.sum(weights, axis=-1)
    summed_new = summed_old * factor[..., None] + jnp.einsum(
        "kgtn,nkd->kgtd",
        weights.astype(jnp.bfloat16),
        value_rows,
        preferred_element_type=jnp.float32,
    )
    return (best_new, total_new, summed_new)


def block_size(piece_rows):
    return math.gcd(piece_rows, 512)


def body(
    hidden_in,
    attn_gain,
    q_weight,
    k_weight,
    v_weight,
    o_weight,
    cache_kv,
    moe_gain,
    expert_in,
    expert_out,
    routes,
    route_prob,
    page_slot,
):
    seq_count = lax.axis_size("seq")
    seq_index = lax.axis_index("seq")
    exp_index = lax.axis_index("exp")
    tokens_here = hidden_in.shape[0]
    head_dim = HEAD_DIM
    kv_local = k_weight.shape[1] // head_dim
    group_size = HEADS // KV_HEADS
    prompt_len = tokens_here * seq_count // 2
    first_row = seq_index * tokens_here
    query_rows = first_row + jnp.arange(tokens_here, dtype=jnp.int32)
    query_second = query_rows >= prompt_len
    holds_first = first_row < prompt_len
    normed = rms_norm(hidden_in, attn_gain)
    queries = jnp.dot(normed, q_weight, preferred_element_type=jnp.float32).astype(jnp.bfloat16)
    keys_new = jnp.dot(normed, k_weight, preferred_element_type=jnp.float32).astype(jnp.bfloat16)
    values_new = jnp.dot(normed, v_weight, preferred_element_type=jnp.float32).astype(jnp.bfloat16)
    pair_width = 2 * kv_local * head_dim
    pairs_new = jnp.stack(
        [
            keys_new.reshape(tokens_here, kv_local, head_dim),
            values_new.reshape(tokens_here, kv_local, head_dim),
        ],
        axis=2,
    ).reshape(tokens_here, pair_width)
    query_heads = queries.reshape(tokens_here, kv_local, group_size, head_dim)
    cache_lines = cache_kv.reshape(tokens_here, -1)
    blocks_here = tokens_here // PAGE
    rounds = blocks_here // seq_count
    outgoing = pairs_new.reshape(rounds, seq_count, PAGE * pair_width)
    received = lax.all_to_all(outgoing, "seq", split_axis=1, concat_axis=1, tiled=True)
    block_ids = (
        jnp.arange(seq_count, dtype=jnp.int32)[None, :] * blocks_here
        + jnp.arange(rounds, dtype=jnp.int32)[:, None] * seq_count
        + seq_index
    ).reshape(-1)
    table_ids = jnp.arange(page_slot.shape[0], dtype=jnp.int32)
    page_slots = jnp.sum(
        jnp.where(block_ids[:, None] == table_ids[None, :], page_slot[None, :], 0), axis=1
    )
    local_pages = (
        jnp.zeros((blocks_here, PAGE * pair_width), jnp.bfloat16)
        .at[page_slots]
        .set(received.reshape(blocks_here, -1))
    )
    page_rows = local_pages.reshape(blocks_here, PAGE, kv_local, 2, head_dim).transpose(
        0, 2, 3, 1, 4
    )
    page_rows = page_rows.reshape(blocks_here, kv_local, 2, PAGE * head_dim)
    start_state = (
        jnp.full((kv_local, group_size, tokens_here), masked_score, jnp.float32),
        jnp.zeros((kv_local, group_size, tokens_here), jnp.float32),
        jnp.zeros((kv_local, group_size, tokens_here, head_dim), jnp.float32),
    )

    def new_keys_part(carried, new_block, key_first):
        width_rows = new_block.shape[0]
        key_rows = key_first + jnp.arange(width_rows, dtype=jnp.int32)
        visible = ((key_rows >= prompt_len)[None, :] == query_second[:, None]) & (
            key_rows[None, :] <= query_rows[:, None]
        )
        split_pairs = new_block.reshape(width_rows, kv_local, 2, head_dim)
        return lax.cond(
            jnp.any(visible),
            lambda carried_in: attend_block(
                carried_in, query_heads, visible, split_pairs[:, :, 0], split_pairs[:, :, 1]
            ),
            lambda carried_in: carried_in,
            carried,
        )

    carried = start_state
    new_piece = lax.all_gather(pairs_new, "seq", axis=0, tiled=True)
    cache_piece = lax.all_gather(cache_lines, "seq", axis=0, tiled=True)
    piece_rows = new_piece.shape[0]
    stride = block_size(piece_rows)
    new_blocks = new_piece.reshape(piece_rows // stride, stride, -1)
    cache_blocks = cache_piece.reshape(piece_rows // stride, 2 * stride, kv_local, 2, head_dim)
    offsets = stride * jnp.arange(piece_rows // stride, dtype=jnp.int32)
    everything = jnp.ones((tokens_here, 2 * stride), bool)

    def visit(carried_in, block_part):
        new_block, cache_block, key_first = block_part
        carried_in = new_keys_part(carried_in, new_block, key_first)
        carried_in = lax.cond(
            holds_first,
            lambda inner: attend_block(
                inner, query_heads, everything, cache_block[:, :, 0], cache_block[:, :, 1]
            ),
            lambda inner: inner,
            carried_in,
        )
        return (carried_in, None)

    carried, _ = lax.scan(visit, carried, (new_blocks, cache_blocks, offsets))
    best_final, total_final, summed_final = carried
    attended = (
        (summed_final / total_final[..., None])
        .transpose(2, 0, 1, 3)
        .reshape(tokens_here, -1)
        .astype(jnp.bfloat16)
    )
    mixed_rows = lax.psum_scatter(
        jnp.dot(attended, o_weight, preferred_element_type=jnp.float32).astype(jnp.bfloat16),
        "exp",
        scatter_dimension=0,
        tiled=True,
    ).astype(jnp.float32)
    moe_rows = mixed_rows.shape[0]
    residual = (
        lax.dynamic_slice_in_dim(hidden_in, exp_index * moe_rows, moe_rows, 0).astype(jnp.float32)
        + residual_scale * mixed_rows
    )
    moe_in = rms_norm(residual, moe_gain)
    top_count = routes.shape[1]
    assigns = moe_rows * top_count
    capacity = 2 * moe_rows * top_count // EXPERTS
    flat_ids = routes.reshape(-1)
    hit_table = (flat_ids[:, None] == jnp.arange(EXPERTS, dtype=jnp.int32)[None, :]).astype(
        jnp.int32
    )
    earlier = jnp.cumsum(hit_table, axis=0) - hit_table
    slot_rank = jnp.sum(earlier * hit_table, axis=1)
    dest_slot = flat_ids * capacity + slot_rank
    source = (
        jnp.full((EXPERTS * capacity,), assigns, jnp.int32)
        .at[dest_slot]
        .set(jnp.arange(assigns, dtype=jnp.int32))
    )
    filled = source < assigns
    picked = moe_in[jnp.minimum(source, assigns - 1) // top_count]
    dispatched = jnp.where(filled[:, None], picked, jnp.zeros_like(picked)).reshape(
        seq_count, EXPERTS // seq_count, capacity, -1
    )
    hidden = jnp.einsum(
        "sexd,edf->sexf",
        lax.all_to_all(dispatched, "seq", split_axis=0, concat_axis=0, tiled=True),
        expert_in,
        preferred_element_type=jnp.float32,
    )
    half_width = hidden.shape[-1] // 2
    active = (jax.nn.silu(hidden[..., :half_width]) * hidden[..., half_width:]).astype(jnp.bfloat16)
    produced = jnp.einsum(
        "sexf,efd->sexd", active, expert_out, preferred_element_type=jnp.float32
    ).astype(jnp.bfloat16)
    returned = lax.all_to_all(produced, "seq", split_axis=0, concat_axis=0, tiled=True)
    flat_back = returned.reshape(EXPERTS * capacity, -1)
    per_assign = flat_back[dest_slot].reshape(moe_rows, top_count, -1)
    share = route_prob / jnp.sum(route_prob, axis=-1, keepdims=True)
    moe = jnp.sum(share[..., None] * per_assign.astype(jnp.float32), axis=1)
    hidden_out = (residual + residual_scale * moe).astype(jnp.bfloat16)
    return (hidden_out, page_rows)


def solution(mesh):
    return jax.shard_map(
        body,
        mesh=mesh,
        in_specs=(
            P("seq", None),
            P(),
            P(None, "exp"),
            P(None, "exp"),
            P(None, "exp"),
            P("exp", None),
            P("seq", "exp"),
            P(),
            P("seq", None, None),
            P("seq", None, None),
            P(("seq", "exp"), None),
            P(("seq", "exp"), None),
            P(),
        ),
        out_specs=(P(("seq", "exp"), None), P("seq", "exp", None, None)),
        check_vma=False,
    )
```

profile of v0, /device:TPU:0, one launch (start us, length us, event | category | flops | bytes accessed | tf_op | source)
XLA Modules:
  0.0 385.0 jit_solution(13722507623709581729)
XLA Ops:
  14.7 40.6 %all-gather.3.cloned.1.call-done = bf16[2048,256]{0,1:T(8,128)(2,1)} async-done(((bf16[256,256]{0,1:T(8,128)(2,1)}), bf16[2048,256]{0,1:T(8,128)(2,1)}) %all-gather.3.cloned.1.call-update) | async-done | bytes 1048592 | tf_op jit(solution)/shard_map/all_gather | solution.py:134
  56.7 49.0 %all-gather.5.cloned.1.call-done = bf16[2048,512]{1,0:T(8,128)(2,1)} async-done(((bf16[256,512]{1,0:T(8,128)(2,1)}), bf16[2048,512]{1,0:T(8,128)(2,1)}) %all-gather.5.cloned.1.call-update) | async-done | bytes 2097168 | tf_op jit(solution)/shard_map/all_gather | solution.py:135
  105.7 8.9 %reshape.173 = bf16[4,1024,2,2,64]{4,3,2,1,0:T(2,128)(2,1)} reshape(bf16[2048,512]{1,0:T(8,128)(2,1)} %all-gather.5.cloned.1.call-done) | data formatting | bytes 4194304 | tf_op jit(solution)/shard_map/reshape | solution.py:139
  114.6 10.6 %copy.101 = bf16[4,1024,2,2,64]{1,4,2,3,0:T(8,128)(2,1)} copy(bf16[4,1024,2,2,64]{4,3,2,1,0:T(2,128)(2,1)} %reshape.173) | data formatting | bytes 4194304
  125.3 35.4 %while.16 = (s32[]{:T(128)}, f32[2,3,256]{2,1,0:T(4,128)S(1)}, f32[2,3,256]{2,1,0:T(4,128)S(1)}, f32[2,3,256,64]{2,3,1,0:T(8,128)S(1)}, pred[]{:T(512)}, /*index...) while((s32[]{:T(128)}, f32[2,3,256]{2,1,0:T(4,128)S(1)}, ...), condition=%wide.region_11.12_spmd.clone.clone, body=%wide.region_1.11_spmd.clone.clone.sunk | while | flops 627712256 | bytes 33374036 | solution.py:156
  129.0 2.5 conditional.8
  131.5 4.5 %conditional.9 = ((f32[2,3,256]{2,1,0:T(4,128)S(1)}, f32[2,3,256]{2,1,0:T(4,128)S(1)}, f32[2,3,256,64]{2,3,1,0:T(8,128)S(1)})) conditional(s32[]{:T(128)} %convert_element_type.152, (f32[2,3,256]{2,1,0:T(4,128)S(1)}, f32[2,3,256]{2,1,0:T(4,128)S(1)}, f32[2,3,256,64]{2,3,1,0:T(8,128)S(1)}) %get-tuple-element.445, ...), branch_computations={%region_7.7_spmd, %region_8.10_spmd} | conditional | flops 415435776 | bytes 21532708 | solution.py:146
  139.7 4.5 %conditional.9 = ((f32[2,3,256]{2,1,0:T(4,128)S(1)}, f32[2,3,256]{2,1,0:T(4,128)S(1)}, f32[2,3,256,64]{2,3,1,0:T(8,128)S(1)})) conditional(s32[]{:T(128)} %convert_element_type.152, (f32[2,3,256]{2,1,0:T(4,128)S(1)}, f32[2,3,256]{2,1,0:T(4,128)S(1)}, f32[2,3,256,64]{2,3,1,0:T(8,128)S(1)}) %get-tuple-element.445, ...), branch_computations={%region_7.7_spmd, %region_8.10_spmd} | conditional | flops 415435776 | bytes 21532708 | solution.py:146
  148.0 4.5 %conditional.9 = ((f32[2,3,256]{2,1,0:T(4,128)S(1)}, f32[2,3,256]{2,1,0:T(4,128)S(1)}, f32[2,3,256,64]{2,3,1,0:T(8,128)S(1)})) conditional(s32[]{:T(128)} %convert_element_type.152, (f32[2,3,256]{2,1,0:T(4,128)S(1)}, f32[2,3,256]{2,1,0:T(4,128)S(1)}, f32[2,3,256,64]{2,3,1,0:T(8,128)S(1)}) %get-tuple-element.445, ...), branch_computations={%region_7.7_spmd, %region_8.10_spmd} | conditional | flops 415435776 | bytes 21532708 | solution.py:146
  156.2 4.5 %conditional.9 = ((f32[2,3,256]{2,1,0:T(4,128)S(1)}, f32[2,3,256]{2,1,0:T(4,128)S(1)}, f32[2,3,256,64]{2,3,1,0:T(8,128)S(1)})) conditional(s32[]{:T(128)} %convert_element_type.152, (f32[2,3,256]{2,1,0:T(4,128)S(1)}, f32[2,3,256]{2,1,0:T(4,128)S(1)}, f32[2,3,256,64]{2,3,1,0:T(8,128)S(1)}) %get-tuple-element.445, ...), branch_computations={%region_7.7_spmd, %region_8.10_spmd} | conditional | flops 415435776 | bytes 21532708 | solution.py:146
  164.3 2.4 scatter_custom_fusion
  166.9 19.4 %reduce-scatter.2.cloned.1.call-done = bf16[64,1536]{1,0:T(8,128)(2,1)} async-done(((bf16[256,1536]{1,0:T(8,128)(2,1)}), bf16[64,1536]{1,0:T(8,128)(2,1)}) %reduce-scatter.2.cloned.1.call-update) | async-done | bytes 196624 | tf_op jit(solution)/shard_map/reduce_scatter | solution.py:164
  188.5 5.6 %gather_fusion = bf16[1024,1536]{1,0:T(8,128)(2,1)} fusion(bf16[64,1536]{1,0:T(8,128)(2,1)S(1)} %multiply_convert_fusion, s32[1024]{0:T(1024)S(1)} %fusion.59), kind=kCustom, calls=%fused_computation | custom fusion | bytes 6295552 | tf_op jit(solution)/shard_map/gather | solution.py:192
  194.1 3.8 broadcast_select_fusion
  197.9 5.8 %all-to-all-start = ((bf16[8,4,32,1536]{3,2,1,0:T(8,128)(2,1)}), bf16[8,4,32,1536]{3,2,1,0:T(8,128)(2,1)}, u32[]{:S(2)}, u32[]{:S(2)}) async-start(bf16[8,4,32,1536]{3,2,1,0:T(8,128)(2,1)} %broadcast_select_fusion), calls=%async_computation.1 | async-start | bytes 6291456 | tf_op jit(solution)/shard_map/all_to_all | solution.py:198
  204.9 69.6 %all-to-all-done = bf16[8,4,32,1536]{3,2,1,0:T(8,128)(2,1)} async-done(((bf16[8,4,32,1536]{3,2,1,0:T(8,128)(2,1)}), bf16[8,4,32,1536]{3,2,1,0:T(8,128)(2,1)}, u32[]{:S(2)}, u32[]{:S(2)}) %all-to-all-start) | async-done | bytes 3145760 | tf_op jit(solution)/shard_map/all_to_all | solution.py:198
  274.5 3.6 all-to-all-start.2
  278.2 7.4 %fusion.39 = f32[8,4,32,1024]{3,2,0,1:T(8,128)S(1)} fusion(bf16[4,1536,1024]{2,1,0:T(8,128)(2,1)} %param.27, bf16[8,4,32,1536]{3,2,1,0:T(8,128)(2,1)} %all-to-all-done), kind=kOutput, calls=%fused_computation.53 | convolution fusion | flops 3221225472 | bytes 19922944 | tf_op jit(solution)/shard_map/sexd,edf->sexf/dot_general | solution.py:196
  285.6 4.6 %fusion.34 = bf16[8,4,32,1536]{3,2,0,1:T(8,128)(2,1)S(1)} fusion(bf16[4,512,1536]{2,1,0:T(8,128)(2,1)} %param.28, f32[8,4,32,1024]{3,2,0,1:T(8,128)S(1)} %fusion.39), kind=kOutput, calls=%fused_computation.47 | convolution fusion | flops 1615331328 | bytes 13631488 | tf_op jit(solution)/shard_map/sexf,efd->sexd/dot_general | solution.py:204
  290.2 1.9 copy.108
  292.1 6.1 %all-to-all-start.1 = ((bf16[8,4,32,1536]{3,2,1,0:T(8,128)(2,1)}), bf16[8,4,32,1536]{3,2,1,0:T(8,128)(2,1)}, u32[]{:S(2)}, u32[]{:S(2)}) async-start(bf16[8,4,32,1536]{3,2,1,0:T(8,128)(2,1)} %copy.108), calls=%async_computation.2 | async-start | bytes 6291456 | tf_op jit(solution)/shard_map/all_to_all | solution.py:207
  301.4 67.3 %all-to-all-done.1 = bf16[8,4,32,1536]{3,2,1,0:T(8,128)(2,1)} async-done(((bf16[8,4,32,1536]{3,2,1,0:T(8,128)(2,1)}), bf16[8,4,32,1536]{3,2,1,0:T(8,128)(2,1)}, u32[]{:S(2)}, u32[]{:S(2)}) %all-to-all-start.1) | async-done | bytes 3145760 | tf_op jit(solution)/shard_map/all_to_all | solution.py:207
  368.7 5.9 %gather_fusion.1 = bf16[512,1536]{1,0:T(8,128)(2,1)S(1)} fusion(bf16[1024,1536]{1,0:T(8,128)(2,1)} %bitcast.33, s32[1024]{0:T(1024)S(1)} %pad_clamp_fusion), kind=kCustom, calls=%fused_computation.1 | custom fusion | bytes 3147776 | tf_op jit(solution)/shard_map/gather | solution.py:209
  374.6 2.2 fusion.37
  (147 shorter events, 52.7 us)
Async XLA Ops:
  7.2 153.6 %copy-start = (bf16[384,1536]{1,0:T(8,128)(2,1)S(1)}, bf16[384,1536]{1,0:T(8,128)(2,1)}, u32[]{:S(2)}) copy-start(bf16[384,1536]{1,0:T(8,128)(2,1)} %param.24) | copy-start | bytes 3538948
  7.2 6.7 %copy-start.1 = (bf16[256,1536]{1,0:T(8,128)(2,1)S(1)}, bf16[256,1536]{1,0:T(8,128)(2,1)}, u32[]{:S(2)}) copy-start(bf16[256,1536]{1,0:T(8,128)(2,1)} %param.19) | copy-start | bytes 2359300
  7.2 6.7 %copy-start.10 = (f32[1536]{0:T(1024)S(1)}, f32[1536]{0:T(1024)}, u32[]{:S(2)}) copy-start(f32[1536]{0:T(1024)} %param.20) | copy-start | bytes 18436
  7.2 5.8 %copy-start.4 = (bf16[512,256]{1,0:T(8,128)(2,1)S(1)}, bf16[512,256]{1,0:T(8,128)(2,1)}, u32[]{:S(2)}) copy-start(bf16[512,256]{1,0:T(8,128)(2,1)} %param.25) | copy-start | bytes 786436
  7.2 6.7 %copy-start.9 = (bf16[1536,384]{1,0:T(8,128)(2,1)S(1)}, bf16[1536,384]{1,0:T(8,128)(2,1)}, u32[]{:S(2)}) copy-start(bf16[1536,384]{1,0:T(8,128)(2,1)} %param.21) | copy-start | bytes 3538948
  7.2 48.1 %all-gather.3.cloned.1.call-start = ((), (), s32[]{:S(2)}) async-start(), calls=%async_computation.4 | async-start | bytes 1179648 | tf_op jit(solution)/shard_map/all_gather | solution.py:134
  13.0 92.7 %all-gather.5.cloned.1.call-start = ((), (), s32[]{:S(2)}) async-start(), calls=%async_computation.5 | async-start | bytes 2359296 | tf_op jit(solution)/shard_map/all_gather | solution.py:135
  13.9 172.4 %reduce-scatter.2.cloned.1.call-start = ((), (), s32[]{:S(2)}) async-start(), calls=%async_computation.6 | async-start | bytes 983040 | tf_op jit(solution)/shard_map/reduce_scatter | solution.py:164
  160.7 1.6 copy-start.5
  160.7 25.6 %copy-start.2 = (bf16[256,1536]{1,0:T(8,128)(2,1)S(1)}, bf16[256,1536]{1,0:T(8,128)(2,1)}, u32[]{:S(2)}) copy-start(bf16[256,1536]{1,0:T(8,128)(2,1)} %param.19) | copy-start | bytes 2359300
  160.7 26.7 %copy-start.7 = (f32[1536]{0:T(1024)S(1)}, f32[1536]{0:T(1024)}, u32[]{:S(2)}) copy-start(f32[1536]{0:T(1024)} %param.26) | copy-start | bytes 18436
  197.9 5.8 %copy-start.3 = (bf16[256,2,2,64]{0,3,2,1:T(8,128)(2,1)S(1)}, bf16[256,2,2,64]{0,3,2,1:T(8,128)(2,1)}, u32[]{:S(2)}) copy-start(bf16[256,2,2,64]{0,3,2,1:T(8,128)(2,1)} %pad_maximum_fusion) | copy-start | bytes 393220
  197.9 76.6 %all-to-all-start = ((bf16[8,4,32,1536]{3,2,1,0:T(8,128)(2,1)}), bf16[8,4,32,1536]{3,2,1,0:T(8,128)(2,1)}, u32[]{:S(2)}, u32[]{:S(2)}) async-start(bf16[8,4,32,1536]{3,2,1,0:T(8,128)(2,1)} %broadcast_select_fusion), calls=%async_computation.1 | async-start | bytes 6291456 | tf_op jit(solution)/shard_map/all_to_all | solution.py:198
  274.5 17.6 %all-to-all-start.2 = ((bf16[4,8,2048]{2,0,1:T(4,128)(2,1)}), bf16[4,8,2048]{2,0,1:T(4,128)(2,1)S(1)}, u32[]{:S(2)}, u32[]{:S(2)}) async-start(bf16[4,8,2048]{2,0,1:T(4,128)(2,1)} %copy.110), calls=%async_computation.3 | async-start | bytes 262144 | tf_op jit(solution)/shard_map/all_to_all | solution.py:92
  292.1 6.1 %copy-start.6 = (f32[64,8]{0,1:T(8,128)S(1)}, f32[64,8]{0,1:T(8,128)}, u32[]{:S(2)}) copy-start(f32[64,8]{0,1:T(8,128)} %param.30) | copy-start | bytes 6148
  292.1 7.1 %copy-start.8 = (s32[256]{0:T(256)S(1)}, s32[256]{0:T(256)}, u32[]{:S(2)}) copy-start(s32[256]{0:T(256)} %param.31) | copy-start | bytes 3076
  292.1 76.6 %all-to-all-start.1 = ((bf16[8,4,32,1536]{3,2,1,0:T(8,128)(2,1)}), bf16[8,4,32,1536]{3,2,1,0:T(8,128)(2,1)}, u32[]{:S(2)}, u32[]{:S(2)}) async-start(bf16[8,4,32,1536]{3,2,1,0:T(8,128)(2,1)} %copy.108), calls=%async_computation.2 | async-start | bytes 6291456 | tf_op jit(solution)/shard_map/all_to_all | solution.py:207
Sparse Core Ops, SparseCore 0:
  13.1 42.2 all-gather.2
  57.5 48.1 all-gather.4
  162.4 23.8 reduce-scatter.1
where the time goes:
time: 386 us; the launch traced here: 385 us
  waiting for transfers between devices  246 us (64%)
  local copies, waits for them, and re-layouts  49.6 us (13%)
  matrix products  28.3 us (7%)
  other arithmetic  28.1 us (7%)
  starting transfers between devices  15.7 us (4%)
  between operations  14.1 us (4%)
    all_to_all x1, waiting for transfers between devices, body(): lax.all_to_all(dispatched, 'seq', split_axis=0, concat_axis=0, tiled=True)  69.6 us
    all_to_all x1, waiting for transfers between devices, body(): lax.all_to_all(produced, 'seq', split_axis=0, concat_axis=0, tiled=True)  67.3 us
    all_gather x1, waiting for transfers between devices, body(): cache_piece = lax.all_gather(cache_lines, 'seq', axis=0, tiled=True)  49 us
    all_gather x1, waiting for transfers between devices, body(): new_piece = lax.all_gather(pairs_new, 'seq', axis=0, tiled=True)  40.6 us
    reduce_scatter x1, waiting for transfers between devices, body(): lax.psum_scatter(jnp.dot(attended, o_weight, preferred_element_type=jnp.f...  19.4 us
    unnamed x26, local copies, waits for them, and re-layouts  11.7 us
    reshape x1, local copies, waits for them, and re-layouts, body(): cache_piece.reshape(piece_rows // stride, 2 * stride, kv_local, 2, head_dim)  8.88 us
  transfers between devices with their start and end apart: 6, of which 5 were waited for; matrix products, arithmetic and copies ran while one was open for 7% of the time, Pallas kernels for 0%

commit v1 on v0

--- a/solution.py
+++ b/solution.py
@@ -131,8 +131,9 @@
         )
 
     carried = start_state
-    new_piece = lax.all_gather(pairs_new, "seq", axis=0, tiled=True)
-    cache_piece = lax.all_gather(cache_lines, "seq", axis=0, tiled=True)
+    formed = jnp.concatenate([pairs_new, cache_lines], 1)
+    opened = lax.all_gather(formed, "seq", axis=0, tiled=True)
+    new_piece, cache_piece = jnp.split(opened, [pairs_new.shape[1]], 1)
     piece_rows = new_piece.shape[0]
     stride = block_size(piece_rows)
     new_blocks = new_piece.reshape(piece_rows // stride, stride, -1)

time: 386 us -> 354 us (0.917)
  waiting for transfers between devices: 246 us -> 217 us
  local copies, waits for them, and re-layouts: 49.6 us -> 44.6 us
    all_gather x2 -> x1, waiting for transfers between devices: 89.6 us -> 61.2 us  [body(): opened = lax.all_gather(formed, 'seq', axis=0, tiled=True)]
    reshape x1, local copies, waits for them, and re-layouts: 8.88 us -> 3.64 us  [body(): cache_piece.reshape(piece_rows // stride, 2 * stride, kv_local, 2, head_dim)]
  transfers between devices with their start and end apart: 6 -> 5, of which waited for: 5 -> 4; matrix products, arithmetic and copies ran while one was open for 7% -> 7% of each run, Pallas kernels for 0% -> 0%
where the time goes in v1:
time: 354 us; the launch traced here: 353 us
  waiting for transfers between devices  217 us (61%)
  local copies, waits for them, and re-layouts  44.6 us (13%)
  matrix products  29.5 us (8%)
  other arithmetic  28.2 us (8%)
  starting transfers between devices  15.5 us (4%)
  between operations  14.4 us (4%)
    all_to_all x1, waiting for transfers between devices, body(): lax.all_to_all(dispatched, 'seq', split_axis=0, concat_axis=0, tiled=True)  69.6 us
    all_to_all x1, waiting for transfers between devices, body(): lax.all_to_all(produced, 'seq', split_axis=0, concat_axis=0, tiled=True)  67.3 us
    all_gather x1, waiting for transfers between devices, body(): opened = lax.all_gather(formed, 'seq', axis=0, tiled=True)  61.2 us
    reduce_scatter x1, waiting for transfers between devices, body(): lax.psum_scatter(jnp.dot(attended, o_weight, preferred_element_type=jnp.f...  19.4 us
    unnamed x26, local copies, waits for them, and re-layouts  11.8 us
    dot_general x1, matrix products, body(): jnp.einsum('sexd,edf->sexf', lax.all_to_all(dispatched, 'seq', split_axis...  7.35 us
  transfers between devices with their start and end apart: 5, of which 4 were waited for; matrix products, arithmetic and copies ran while one was open for 7% of the time, Pallas kernels for 0%

profile of v1, /device:TPU:0, one launch (start us, length us, event | category | flops | bytes accessed | tf_op | source)
XLA Modules:
  0.0 353.1 jit_solution(13614838724813605585)
XLA Ops:
  13.4 1.9 convolution_convert_fusion.1
  15.5 61.2 %all-gather.2.cloned.1.call-done = bf16[2048,768]{1,0:T(8,128)(2,1)} async-done(((bf16[256,768]{1,0:T(8,128)(2,1)}), bf16[2048,768]{1,0:T(8,128)(2,1)}) %all-gather.2.cloned.1.call-update) | async-done | bytes 3145744 | tf_op jit(solution)/shard_map/all_gather | solution.py:135
  78.2 3.6 %reshape.173 = bf16[4,1024,2,2,64]{4,3,2,1,0:T(2,128)(2,1)} reshape(bf16[2048,512]{1,0:T(8,128)(2,1)S(1)} %slice-done) | data formatting | bytes 4194304 | tf_op jit(solution)/shard_map/reshape | solution.py:140
  81.8 10.7 %copy.105 = bf16[4,1024,2,2,64]{1,4,2,3,0:T(8,128)(2,1)} copy(bf16[4,1024,2,2,64]{4,3,2,1,0:T(2,128)(2,1)} %reshape.173) | data formatting | bytes 4194304
  92.6 36.0 %while.16 = (s32[]{:T(128)}, f32[2,3,256]{2,1,0:T(4,128)S(1)}, f32[2,3,256]{2,1,0:T(4,128)S(1)}, f32[2,3,256,64]{2,3,1,0:T(8,128)S(1)}, pred[]{:T(512)}, /*index...) while((s32[]{:T(128)}, f32[2,3,256]{2,1,0:T(4,128)S(1)}, ...), condition=%wide.region_11.12_spmd.clone.clone, body=%wide.region_1.11_spmd.clone.clone.sunk | while | flops 627712256 | bytes 33898324 | solution.py:157
  96.5 2.5 conditional.8
  99.0 4.5 %conditional.9 = ((f32[2,3,256]{2,1,0:T(4,128)S(1)}, f32[2,3,256]{2,1,0:T(4,128)S(1)}, f32[2,3,256,64]{2,3,1,0:T(8,128)S(1)})) conditional(s32[]{:T(128)} %convert_element_type.152, (f32[2,3,256]{2,1,0:T(4,128)S(1)}, f32[2,3,256]{2,1,0:T(4,128)S(1)}, f32[2,3,256,64]{2,3,1,0:T(8,128)S(1)}) %get-tuple-element.445, ...), branch_computations={%region_7.7_spmd, %region_8.10_spmd} | conditional | flops 415435776 | bytes 21532708 | solution.py:147
  107.4 4.5 %conditional.9 = ((f32[2,3,256]{2,1,0:T(4,128)S(1)}, f32[2,3,256]{2,1,0:T(4,128)S(1)}, f32[2,3,256,64]{2,3,1,0:T(8,128)S(1)})) conditional(s32[]{:T(128)} %convert_element_type.152, (f32[2,3,256]{2,1,0:T(4,128)S(1)}, f32[2,3,256]{2,1,0:T(4,128)S(1)}, f32[2,3,256,64]{2,3,1,0:T(8,128)S(1)}) %get-tuple-element.445, ...), branch_computations={%region_7.7_spmd, %region_8.10_spmd} | conditional | flops 415435776 | bytes 21532708 | solution.py:147
  115.8 4.5 %conditional.9 = ((f32[2,3,256]{2,1,0:T(4,128)S(1)}, f32[2,3,256]{2,1,0:T(4,128)S(1)}, f32[2,3,256,64]{2,3,1,0:T(8,128)S(1)})) conditional(s32[]{:T(128)} %convert_element_type.152, (f32[2,3,256]{2,1,0:T(4,128)S(1)}, f32[2,3,256]{2,1,0:T(4,128)S(1)}, f32[2,3,256,64]{2,3,1,0:T(8,128)S(1)}) %get-tuple-element.445, ...), branch_computations={%region_7.7_spmd, %region_8.10_spmd} | conditional | flops 415435776 | bytes 21532708 | solution.py:147
  124.2 4.5 %conditional.9 = ((f32[2,3,256]{2,1,0:T(4,128)S(1)}, f32[2,3,256]{2,1,0:T(4,128)S(1)}, f32[2,3,256,64]{2,3,1,0:T(8,128)S(1)})) conditional(s32[]{:T(128)} %convert_element_type.152, (f32[2,3,256]{2,1,0:T(4,128)S(1)}, f32[2,3,256]{2,1,0:T(4,128)S(1)}, f32[2,3,256,64]{2,3,1,0:T(8,128)S(1)}) %get-tuple-element.445, ...), branch_computations={%region_7.7_spmd, %region_8.10_spmd} | conditional | flops 415435776 | bytes 21532708 | solution.py:147
  132.3 2.4 scatter_custom_fusion
  134.9 19.4 %reduce-scatter.2.cloned.1.call-done = bf16[64,1536]{1,0:T(8,128)(2,1)} async-done(((bf16[256,1536]{1,0:T(8,128)(2,1)}), bf16[64,1536]{1,0:T(8,128)(2,1)}) %reduce-scatter.2.cloned.1.call-update) | async-done | bytes 196624 | tf_op jit(solution)/shard_map/reduce_scatter | solution.py:165
  156.4 5.6 %gather_fusion = bf16[1024,1536]{1,0:T(8,128)(2,1)} fusion(bf16[64,1536]{1,0:T(8,128)(2,1)S(1)} %multiply_convert_fusion, s32[1024]{0:T(1024)S(1)} %fusion.59), kind=kCustom, calls=%fused_computation | custom fusion | bytes 6295552 | tf_op jit(solution)/shard_map/gather | solution.py:193
  162.0 3.8 %broadcast_select_fusion = bf16[8,4,32,1536]{3,2,1,0:T(8,128)(2,1)} fusion(bf16[8,4,32,1536]{3,2,1,0:T(8,128)(2,1)} %bitcast.138, pred[8,4,32]{2,1,0:T(4,128)(4,1)S(1)} %broadcast_in_dim.86), kind=kLoop, calls=%fused_computation.51 | loop fusion | flops 1572864 | bytes 6292480 | tf_op jit(solution)/shard_map/jit(_where)/select_n | solution.py:194
  165.8 5.7 %all-to-all-start = ((bf16[8,4,32,1536]{3,2,1,0:T(8,128)(2,1)}), bf16[8,4,32,1536]{3,2,1,0:T(8,128)(2,1)}, u32[]{:S(2)}, u32[]{:S(2)}) async-start(bf16[8,4,32,1536]{3,2,1,0:T(8,128)(2,1)} %broadcast_select_fusion), calls=%async_computation.1 | async-start | bytes 6291456 | tf_op jit(solution)/shard_map/all_to_all | solution.py:199
  172.7 69.6 %all-to-all-done = bf16[8,4,32,1536]{3,2,1,0:T(8,128)(2,1)} async-done(((bf16[8,4,32,1536]{3,2,1,0:T(8,128)(2,1)}), bf16[8,4,32,1536]{3,2,1,0:T(8,128)(2,1)}, u32[]{:S(2)}, u32[]{:S(2)}) %all-to-all-start) | async-done | bytes 3145760 | tf_op jit(solution)/shard_map/all_to_all | solution.py:199
  242.3 3.6 %all-to-all-start.2 = ((bf16[4,8,2048]{2,0,1:T(4,128)(2,1)}), bf16[4,8,2048]{2,0,1:T(4,128)(2,1)S(1)}, u32[]{:S(2)}, u32[]{:S(2)}) async-start(bf16[4,8,2048]{2,0,1:T(4,128)(2,1)} %copy.114), calls=%async_computation.3 | async-start | bytes 262144 | tf_op jit(solution)/shard_map/all_to_all | solution.py:92
  245.9 7.4 %fusion.39 = f32[8,4,32,1024]{3,2,0,1:T(8,128)S(1)} fusion(bf16[4,1536,1024]{2,1,0:T(8,128)(2,1)} %param.27, bf16[8,4,32,1536]{3,2,1,0:T(8,128)(2,1)} %all-to-all-done), kind=kOutput, calls=%fused_computation.53 | convolution fusion | flops 3221225472 | bytes 19922944 | tf_op jit(solution)/shard_map/sexd,edf->sexf/dot_general | solution.py:197
  253.3 4.6 %fusion.34 = bf16[8,4,32,1536]{3,2,0,1:T(8,128)(2,1)S(1)} fusion(bf16[4,512,1536]{2,1,0:T(8,128)(2,1)} %param.28, f32[8,4,32,1024]{3,2,0,1:T(8,128)S(1)} %fusion.39), kind=kOutput, calls=%fused_computation.47 | convolution fusion | flops 1615331328 | bytes 13631488 | tf_op jit(solution)/shard_map/sexf,efd->sexd/dot_general | solution.py:205
  257.9 1.9 copy.112
  259.9 6.1 %all-to-all-start.1 = ((bf16[8,4,32,1536]{3,2,1,0:T(8,128)(2,1)}), bf16[8,4,32,1536]{3,2,1,0:T(8,128)(2,1)}, u32[]{:S(2)}, u32[]{:S(2)}) async-start(bf16[8,4,32,1536]{3,2,1,0:T(8,128)(2,1)} %copy.112), calls=%async_computation.2 | async-start | bytes 6291456 | tf_op jit(solution)/shard_map/all_to_all | solution.py:208
  269.1 67.3 %all-to-all-done.1 = bf16[8,4,32,1536]{3,2,1,0:T(8,128)(2,1)} async-done(((bf16[8,4,32,1536]{3,2,1,0:T(8,128)(2,1)}), bf16[8,4,32,1536]{3,2,1,0:T(8,128)(2,1)}, u32[]{:S(2)}, u32[]{:S(2)}) %all-to-all-start.1) | async-done | bytes 3145760 | tf_op jit(solution)/shard_map/all_to_all | solution.py:208
  336.4 5.9 %gather_fusion.1 = bf16[512,1536]{1,0:T(8,128)(2,1)S(1)} fusion(bf16[1024,1536]{1,0:T(8,128)(2,1)} %bitcast.34, s32[1024]{0:T(1024)S(1)} %pad_clamp_fusion), kind=kCustom, calls=%fused_computation.1 | custom fusion | bytes 3147776 | tf_op jit(solution)/shard_map/gather | solution.py:210
  342.3 2.2 fusion.37
  (153 shorter events, 52.4 us)
Async XLA Ops:
  7.2 121.6 %copy-start = (bf16[384,1536]{1,0:T(8,128)(2,1)S(1)}, bf16[384,1536]{1,0:T(8,128)(2,1)}, u32[]{:S(2)}) copy-start(bf16[384,1536]{1,0:T(8,128)(2,1)} %param.24) | copy-start | bytes 3538948
  7.2 6.2 %copy-start.1 = (bf16[256,1536]{1,0:T(8,128)(2,1)S(1)}, bf16[256,1536]{1,0:T(8,128)(2,1)}, u32[]{:S(2)}) copy-start(bf16[256,1536]{1,0:T(8,128)(2,1)} %param.19) | copy-start | bytes 2359300
  7.2 6.2 %copy-start.10 = (f32[1536]{0:T(1024)S(1)}, f32[1536]{0:T(1024)}, u32[]{:S(2)}) copy-start(f32[1536]{0:T(1024)} %param.20) | copy-start | bytes 18436
  7.2 5.2 %copy-start.5 = (bf16[512,256]{1,0:T(8,128)(2,1)S(1)}, bf16[512,256]{1,0:T(8,128)(2,1)}, u32[]{:S(2)}) copy-start(bf16[512,256]{1,0:T(8,128)(2,1)} %param.25) | copy-start | bytes 786436
  7.2 69.4 %all-gather.2.cloned.1.call-start = ((), (), s32[]{:S(2)}) async-start(), calls=%async_computation.4 | async-start | bytes 3538944 | tf_op jit(solution)/shard_map/all_gather | solution.py:135
  12.3 3.2 copy-start.3
  13.3 140.9 %reduce-scatter.2.cloned.1.call-start = ((), (), s32[]{:S(2)}) async-start(), calls=%async_computation.5 | async-start | bytes 983040 | tf_op jit(solution)/shard_map/reduce_scatter | solution.py:165
  76.6 1.6 slice-start
  81.8 10.8 %slice-start.1 = ((bf16[2048,768]{1,0:T(8,128)(2,1)}), bf16[2048,256]{1,0:T(8,128)(2,1)S(1)}, s32[]{:S(2)}) async-start(bf16[2048,768]{1,0:T(8,128)(2,1)} %all-gather.2.cloned.1.call-done), calls=%async_computation.7 | async-start | bytes 2097152 | tf_op jit(solution)/shard_map/split | solution.py:136
  128.7 1.6 copy-start.6
  128.7 25.6 %copy-start.2 = (bf16[256,1536]{1,0:T(8,128)(2,1)S(1)}, bf16[256,1536]{1,0:T(8,128)(2,1)}, u32[]{:S(2)}) copy-start(bf16[256,1536]{1,0:T(8,128)(2,1)} %param.19) | copy-start | bytes 2359300
  128.7 26.7 %copy-start.8 = (f32[1536]{0:T(1024)S(1)}, f32[1536]{0:T(1024)}, u32[]{:S(2)}) copy-start(f32[1536]{0:T(1024)} %param.26) | copy-start | bytes 18436
  165.8 5.7 %copy-start.4 = (bf16[256,2,2,64]{0,3,2,1:T(8,128)(2,1)S(1)}, bf16[256,2,2,64]{0,3,2,1:T(8,128)(2,1)}, u32[]{:S(2)}) copy-start(bf16[256,2,2,64]{0,3,2,1:T(8,128)(2,1)} %copy-done.3) | copy-start | bytes 393220
  165.8 76.5 %all-to-all-start = ((bf16[8,4,32,1536]{3,2,1,0:T(8,128)(2,1)}), bf16[8,4,32,1536]{3,2,1,0:T(8,128)(2,1)}, u32[]{:S(2)}, u32[]{:S(2)}) async-start(bf16[8,4,32,1536]{3,2,1,0:T(8,128)(2,1)} %broadcast_select_fusion), calls=%async_computation.1 | async-start | bytes 6291456 | tf_op jit(solution)/shard_map/all_to_all | solution.py:199
  242.3 17.5 %all-to-all-start.2 = ((bf16[4,8,2048]{2,0,1:T(4,128)(2,1)}), bf16[4,8,2048]{2,0,1:T(4,128)(2,1)S(1)}, u32[]{:S(2)}, u32[]{:S(2)}) async-start(bf16[4,8,2048]{2,0,1:T(4,128)(2,1)} %copy.114), calls=%async_computation.3 | async-start | bytes 262144 | tf_op jit(solution)/shard_map/all_to_all | solution.py:92
  259.8 6.1 %copy-start.7 = (f32[64,8]{0,1:T(8,128)S(1)}, f32[64,8]{0,1:T(8,128)}, u32[]{:S(2)}) copy-start(f32[64,8]{0,1:T(8,128)} %param.30) | copy-start | bytes 6148
  259.8 7.1 %copy-start.9 = (s32[256]{0:T(256)S(1)}, s32[256]{0:T(256)}, u32[]{:S(2)}) copy-start(s32[256]{0:T(256)} %param.31) | copy-start | bytes 3076
  259.9 76.6 %all-to-all-start.1 = ((bf16[8,4,32,1536]{3,2,1,0:T(8,128)(2,1)}), bf16[8,4,32,1536]{3,2,1,0:T(8,128)(2,1)}, u32[]{:S(2)}, u32[]{:S(2)}) async-start(bf16[8,4,32,1536]{3,2,1,0:T(8,128)(2,1)} %copy.112), calls=%async_computation.2 | async-start | bytes 6291456 | tf_op jit(solution)/shard_map/all_to_all | solution.py:208
Sparse Core Ops, SparseCore 0:
  13.4 63.1 all-gather.1
  130.4 23.8 reduce-scatter.1
